TPU v7x, 256 devices: a whole 4x4x8 slice. The times are simulated.
256 devices in a mesh: rows: 16 (over x, y), sub: 16 (over z, core).
Axes of the slice: x: 4, y: 4, z: 8, core: 2. Of those that a mesh axis runs over, the one named last changes fastest.
Arguments:
- embeddings: bfloat16 [65536, 1024], P(('rows', 'sub'))
- codes: int32 [64, 65536], P(None, ('rows', 'sub')), may hold values from 0 to 255
- codebook: bfloat16 [256, 1024], P(None, 'sub'), may hold values from -6 to 6
Outputs:
- rotation: float32 [1024, 1024], P('sub')
- rotated: bfloat16 [65536, 1024], P(('rows', 'sub'))
- new_codebook: float32 [256, 1024], P(None, 'sub')
All inputs are finite; a program needn't handle non-finite values.
Results may differ from a plain program's by a relative error of at most 0.0095.
Values may be sent and summed in bfloat16 or wider, within the bound.
No kernel may reach another device: no remote copies, remote signals or barrier semaphores. Data moves between devices by JAX's collectives and lax.ppermute only.
A program may use at most 64 MiB of HBM per device.

v0:
```python
import math
import jax
import jax.numpy as jnp
from jax import lax
from jax.sharding import PartitionSpec as P

NS_STEPS = 3
coef_a = 3.4445
coef_b = -4.775
coef_c = 2.0315
frob_eps = 1e-07


def one_hot_codes(code_block, count_codes):
    levels = lax.broadcasted_iota(jnp.int32, code_block.shape + (count_codes,), 2)
    return (code_block[:, :, None] == levels).astype(jnp.bfloat16)


def decode_rows(codes, table):
    subspaces, local_rows = codes.shape
    count_codes, row_width = table.shape
    sub_width = row_width // subspaces
    codewords = table.reshape(count_codes, subspaces, sub_width)
    one_hot = one_hot_codes(codes, count_codes)
    picked = jnp.einsum("mnk,kmj->nmj", one_hot, codewords, preferred_element_type=jnp.float32)
    return picked.reshape(local_rows, row_width).astype(jnp.bfloat16)


def codeword_totals(codes, row_values, count_codes):
    subspaces, local_rows = codes.shape
    row_width = row_values.shape[1]
    sub_width = row_width // subspaces
    one_hot = one_hot_codes(codes, count_codes)
    pieces = row_values.reshape(local_rows, subspaces, sub_width)
    code_sums = jnp.einsum("mnk,nmj->kmj", one_hot, pieces, preferred_element_type=jnp.float32)
    counts = jnp.sum(one_hot, axis=1, dtype=jnp.float32).T
    return (code_sums.reshape(count_codes, row_width), counts)


def bdot(left, right, dims):
    return lax.dot_general(
        left.astype(jnp.bfloat16),
        right.astype(jnp.bfloat16),
        (dims, ((), ())),
        preferred_element_type=jnp.float32,
    )


def newton_step(z):
    z_half = z.astype(jnp.bfloat16)
    gram = bdot(z_half, z_half, ((1,), (1,)))
    quartic = bdot(gram, gram, ((1,), (0,)))
    mixer = coef_b * gram + coef_c * quartic
    return coef_a * z + bdot(mixer, z_half, ((1,), (0,)))


def body(embeddings, codes, codebook):
    table = lax.all_gather(codebook, "sub", axis=1, tiled=True)
    decoded = decode_rows(codes, table)
    partial = lax.dot_general(
        embeddings, decoded, (((0,), (0,)), ((), ())), preferred_element_type=jnp.float32
    )
    cross = lax.psum(partial, ("rows", "sub"))
    frob_scale = jnp.sqrt(jnp.sum(cross * cross)) + frob_eps
    z = cross / frob_scale
    for newton_step_index in range(NS_STEPS):
        z = newton_step(z)
    rotation_half = z.astype(jnp.bfloat16)
    rotated = jnp.dot(embeddings, rotation_half, preferred_element_type=jnp.float32).astype(
        jnp.bfloat16
    )
    code_sums, counts = codeword_totals(codes, rotated, table.shape[0])
    code_sums = lax.psum(code_sums, ("rows", "sub"))
    counts = lax.psum(counts, ("rows", "sub"))
    me = lax.axis_index("sub")
    cols = codebook.shape[1]
    own_subspaces = counts.shape[1] * cols // code_sums.shape[1]
    own_sums = lax.dynamic_slice_in_dim(code_sums, me * cols, cols, axis=1)
    own_counts = lax.dynamic_slice_in_dim(counts, me * own_subspaces, own_subspaces, axis=1)
    own_codebook = codebook.astype(jnp.float32)
    spread = jnp.repeat(own_counts, cols // own_subspaces, axis=1)
    new_codebook = (own_sums + own_codebook) / (spread + 1.0)
    panel_rows = z.shape[0] // lax.axis_size("sub")
    panel = lax.dynamic_slice_in_dim(z, me * panel_rows, panel_rows, axis=0)
    return (panel, rotated, new_codebook)


def solution(mesh):
    in_specs = (P(("rows", "sub"), None), P(None, ("rows", "sub")), P(None, "sub"))
    out_specs = (P("sub", None), P(("rows", "sub"), None), P(None, "sub"))
    return jax.shard_map(body, mesh=mesh, in_specs=in_specs, out_specs=out_specs, check_vma=False)
```

profile of v0, /device:TPU:6, one launch (start us, length us, event | category | flops | bytes accessed | tf_op | source)
XLA Modules:
  0.0 650.9 jit_solution(6691471587485620089)
XLA Ops:
  7.2 0.0 copy-start
  7.2 0.0 all-reduce.4.cloned.1.call-start
  7.2 21.8 %all_gather.3 = bf16[256,1024]{0,1:T(8,128)(2,1)S(1)} all-gather(bf16[256,64]{0,1:T(8,128)(2,1)} %param.5), channel_id=1, replica_groups=mesh['rows'=16,'sub'=16] {'sub'}, dimensions={1}, use_global_device_ids=true | all-gather | bytes 557056 | tf_op jit(solution)/shard_map/all_gather | solution.py:58
  29.0 5.3 fusion.14
  34.3 0.0 copy-done
  34.3 2.7 convolution_bitcast_fusion
  36.9 0.0 copy-start.2
  36.9 0.0 all-reduce.4.cloned.1.call-update
  37.0 0.0 all-reduce.6.cloned.1.call-start
  37.0 0.8 copy-done.2
  37.8 3.4 convert_reduce_fusion
  41.2 264.1 %all-reduce.4.cloned.1.call-done = f32[1024,1024]{0,1:T(8,128)} async-done(((f32[1024,1024]{0,1:T(8,128)}), f32[1024,1024]{0,1:T(8,128)}) %all-reduce.4.cloned.1.call-update) | async-done | bytes 4194320 | tf_op jit(solution)/shard_map/psum | solution.py:63
  305.3 3.9 multiply_reduce_fusion
  309.9 7.8 %fusion.28 = f32[1024,1024]{1,0:T(8,128)} fusion(f32[1024,1024]{0,1:T(8,128)} %all-reduce.4.cloned.1.call-done, f32[]{:T(128)S(6)} %add.47), kind=kOutput, calls=%fused_computation.30 | convolution fusion | flops 2149580800 | bytes 8388612 | tf_op jit(solution)/shard_map/dot_general | solution.py:41
  317.7 13.9 %multiply_add_fusion.2 = f32[1024,1024]{0,1:T(8,128)} fusion(f32[1024,1024]{0,1:T(8,128)} %all-reduce.4.cloned.1.call-done, f32[]{:T(128)S(6)} %add.47, f32[1024,1024]{1,0:T(8,128)} %fusion.28), kind=kOutput, calls=%fused_computation.12 | convolution fusion | flops 4305453056 | bytes 12582916 | tf_op jit(solution)/shard_map/dot_general | solution.py:41
  331.6 7.8 %fusion.21 = f32[1024,1024]{1,0:T(8,128)} fusion(f32[1024,1024]{0,1:T(8,128)} %multiply_add_fusion.2), kind=kOutput, calls=%fused_computation.28 | convolution fusion | flops 2148532224 | bytes 8388608 | tf_op jit(solution)/shard_map/dot_general | solution.py:41
  339.4 13.7 %multiply_add_fusion.1 = f32[1024,1024]{0,1:T(8,128)} fusion(f32[1024,1024]{0,1:T(8,128)} %multiply_add_fusion.2, f32[1024,1024]{1,0:T(8,128)} %fusion.21), kind=kOutput, calls=%fused_computation.10 | convolution fusion | flops 4303355904 | bytes 12582912 | tf_op jit(solution)/shard_map/dot_general | solution.py:41
  353.1 8.0 %fusion.18 = f32[1024,1024]{1,0:T(8,128)} fusion(f32[1024,1024]{0,1:T(8,128)} %multiply_add_fusion.1), kind=kOutput, calls=%fused_computation.25 | convolution fusion | flops 2148532224 | bytes 8388608 | tf_op jit(solution)/shard_map/dot_general | solution.py:41
  361.2 13.9 %multiply_add_fusion = f32[1024,1024]{0,1:T(8,128)} fusion(f32[1024,1024]{0,1:T(8,128)} %multiply_add_fusion.1, f32[1024,1024]{1,0:T(8,128)} %fusion.18), kind=kOutput, calls=%fused_computation.8 | convolution fusion | flops 4303355904 | bytes 12582912 | tf_op jit(solution)/shard_map/dot_general | solution.py:41
  375.1 2.9 fusion.11
  378.0 0.0 copy-start.1
  378.0 5.1 fusion.1
  383.1 0.0 all-reduce.6.cloned.1.call-update
  383.1 1.2 constant_dynamic-slice_fusion
  384.4 0.9 copy.9
  385.3 1.0 copy.10
  386.3 255.6 %all-reduce.6.cloned.1.call-done = (f32[256,1024]{0,1:T(8,128)}, f32[256,64]{0,1:T(8,128)}) async-done(((f32[256,1024]{0,1:T(8,128)}, f32[256,64]{0,1:T(8,128)}), (f32[256,1024]{0,1:T(8,128)}, f32[256,64]{0,1:T(8,128)})) %all-reduce.6.cloned.1.call-update) | async-done | bytes 1114128 | tf_op jit(solution)/shard_map/psum | solution.py:73
  641.9 0.7 dynamic-slice_add_fusion
  642.6 0.0 copy-done.1
  642.6 1.5 bitcast_divide_fusion
Async XLA Ops:
  7.2 27.1 %copy-start = (bf16[256,1024]{1,0:T(8,128)(2,1)S(1)}, bf16[256,1024]{1,0:T(8,128)(2,1)}, u32[]{:S(2)}) copy-start(bf16[256,1024]{1,0:T(8,128)(2,1)} %param.3) | copy-start | bytes 1572868
  7.2 298.1 %all-reduce.4.cloned.1.call-start = ((), (), s32[]{:S(2)}) async-start(), calls=%async_computation | async-start | bytes 8388608 | tf_op jit(solution)/shard_map/psum | solution.py:63
  36.9 0.8 copy-start.2
  37.0 604.9 %all-reduce.6.cloned.1.call-start = ((), (), s32[]{:S(2)}) async-start(), calls=%async_computation.1 | async-start | bytes 2228224 | tf_op jit(solution)/shard_map/psum | solution.py:73
  378.0 264.6 %copy-start.1 = (bf16[256,64]{0,1:T(8,128)(2,1)S(1)}, bf16[256,64]{0,1:T(8,128)(2,1)}, u32[]{:S(2)}) copy-start(bf16[256,64]{0,1:T(8,128)(2,1)} %param.5) | copy-start | bytes 98308
Sparse Core Ops, SparseCore 0:
  37.1 268.1 all-reduce.3
  383.3 258.5 all-reduce.5
where the time goes:
time: 652 us; the launch traced here: 651 us
  waiting for transfers between devices  520 us (80%)
  matrix products  81.1 us (12%)
  blocking collectives  21.8 us (3%)
  between operations  14.8 us (2%)
  other arithmetic  9.48 us (1%)
    psum x1, waiting for transfers between devices, body(): cross = lax.psum(partial, ('rows', 'sub'))  264 us
    psum x1, waiting for transfers between devices, body(): code_sums = lax.psum(code_sums, ('rows', 'sub'))  256 us
    dot_general x6, matrix products, bdot(): lax.dot_general(left.astype(jnp.bfloat16), right.astype(jnp.bfloat16), (d...  65.2 us
    all_gather x1, blocking collectives, body(): table = lax.all_gather(codebook, 'sub', axis=1, tiled=True)  21.8 us
  transfers between devices with their start and end apart: 2, of which 2 were waited for; matrix products, arithmetic and copies ran while one was open for 1% of the time, Pallas kernels for 0%

commit v1 on v0

--- a/solution.py
+++ b/solution.py
@@ -55,7 +55,9 @@
 
 
 def body(embeddings, codes, codebook):
-    table = lax.all_gather(codebook, "sub", axis=1, tiled=True)
+    table = jnp.concatenate(
+        lax.all_to_all(jnp.stack([codebook] * lax.axis_size("sub")), "sub", 0, 0), axis=1
+    )
     decoded = decode_rows(codes, table)
     partial = lax.dot_general(
         embeddings, decoded, (((0,), (0,)), ((), ())), preferred_element_type=jnp.float32

time: 652 us -> 655 us (level)
    all_to_all x0 -> x1, blocking collectives: none -> 24.3 us  [body(): lax.all_to_all(jnp.stack([codebook] * lax.axis_size('sub')), 'sub', 0, 0)]
    all_gather x1 -> x0, blocking collectives: 21.8 us -> none  [body(): table = lax.all_gather(codebook, 'sub', axis=1, tiled=True)]
where the time goes in v1:
time: 655 us
  waiting for transfers between devices  520 us (79%)
  matrix products  81.1 us (12%)
  blocking collectives  24.3 us (4%)
  between operations  14.8 us (2%)
  other arithmetic  9.48 us (1%)
    psum x1, waiting for transfers between devices, body(): cross = lax.psum(partial, ('rows', 'sub'))  265 us
    psum x1, waiting for transfers between devices, body(): code_sums = lax.psum(code_sums, ('rows', 'sub'))  255 us
    dot_general x6, matrix products, bdot(): lax.dot_general(left.astype(jnp.bfloat16), right.astype(jnp.bfloat16), (d...  65.2 us
    all_to_all x1, blocking collectives, body(): lax.all_to_all(jnp.stack([codebook] * lax.axis_size('sub')), 'sub', 0, 0)  24.3 us
  transfers between devices with their start and end apart: 2, of which 2 were waited for; matrix products, arithmetic and copies ran while one was open for 1% of the time, Pallas kernels for 0%

profile of v1, /device:TPU:6, one launch (start us, length us, event | category | flops | bytes accessed | tf_op | source)
XLA Modules:
  0.0 654.6 jit_solution(3827931222654374977)
XLA Ops:
  7.2 0.0 copy-start
  7.2 0.0 all-reduce.4.cloned.1.call-start
  7.2 0.9 stack.2
  8.1 24.3 %all_to_all.5 = bf16[16,256,64]{1,2,0:T(8,128)(2,1)S(1)} all-to-all(bf16[16,256,64]{1,2,0:T(8,128)(2,1)S(1)} %stack.2), channel_id=1, replica_groups=mesh['rows'=16,'sub'=16] {'sub'}, dimensions={0} | all-to-all | bytes 1048576 | tf_op jit(solution)/shard_map/all_to_all | solution.py:59
  32.4 5.3 fusion.14
  37.7 0.0 copy-done
  37.7 2.7 convolution_bitcast_fusion
  40.3 0.0 copy-start.2
  40.3 0.0 all-reduce.4.cloned.1.call-update
  40.3 0.0 all-reduce.6.cloned.1.call-start
  40.4 0.8 copy-done.2
  41.1 3.4 convert_reduce_fusion
  44.6 264.6 %all-reduce.4.cloned.1.call-done = f32[1024,1024]{0,1:T(8,128)} async-done(((f32[1024,1024]{0,1:T(8,128)}), f32[1024,1024]{0,1:T(8,128)}) %all-reduce.4.cloned.1.call-update) | async-done | bytes 4194320 | tf_op jit(solution)/shard_map/psum | solution.py:65
  309.2 3.9 multiply_reduce_fusion
  313.8 7.8 %fusion.28 = f32[1024,1024]{1,0:T(8,128)} fusion(f32[1024,1024]{0,1:T(8,128)} %all-reduce.4.cloned.1.call-done, f32[]{:T(128)S(6)} %add.47), kind=kOutput, calls=%fused_computation.30 | convolution fusion | flops 2149580800 | bytes 8388612 | tf_op jit(solution)/shard_map/dot_general | solution.py:41
  321.6 13.9 %multiply_add_fusion.2 = f32[1024,1024]{0,1:T(8,128)} fusion(f32[1024,1024]{0,1:T(8,128)} %all-reduce.4.cloned.1.call-done, f32[]{:T(128)S(6)} %add.47, f32[1024,1024]{1,0:T(8,128)} %fusion.28), kind=kOutput, calls=%fused_computation.12 | convolution fusion | flops 4305453056 | bytes 12582916 | tf_op jit(solution)/shard_map/dot_general | solution.py:41
  335.5 7.8 %fusion.21 = f32[1024,1024]{1,0:T(8,128)} fusion(f32[1024,1024]{0,1:T(8,128)} %multiply_add_fusion.2), kind=kOutput, calls=%fused_computation.28 | convolution fusion | flops 2148532224 | bytes 8388608 | tf_op jit(solution)/shard_map/dot_general | solution.py:41
  343.3 13.7 %multiply_add_fusion.1 = f32[1024,1024]{0,1:T(8,128)} fusion(f32[1024,1024]{0,1:T(8,128)} %multiply_add_fusion.2, f32[1024,1024]{1,0:T(8,128)} %fusion.21), kind=kOutput, calls=%fused_computation.10 | convolution fusion | flops 4303355904 | bytes 12582912 | tf_op jit(solution)/shard_map/dot_general | solution.py:41
  357.0 8.0 %fusion.18 = f32[1024,1024]{1,0:T(8,128)} fusion(f32[1024,1024]{0,1:T(8,128)} %multiply_add_fusion.1), kind=kOutput, calls=%fused_computation.25 | convolution fusion | flops 2148532224 | bytes 8388608 | tf_op jit(solution)/shard_map/dot_general | solution.py:41
  365.1 13.9 %multiply_add_fusion = f32[1024,1024]{0,1:T(8,128)} fusion(f32[1024,1024]{0,1:T(8,128)} %multiply_add_fusion.1, f32[1024,1024]{1,0:T(8,128)} %fusion.18), kind=kOutput, calls=%fused_computation.8 | convolution fusion | flops 4303355904 | bytes 12582912 | tf_op jit(solution)/shard_map/dot_general | solution.py:41
  379.0 2.9 fusion.11
  381.9 0.0 copy-start.1
  381.9 5.1 fusion.1
  387.0 0.0 all-reduce.6.cloned.1.call-update
  387.0 1.2 constant_dynamic-slice_fusion
  388.3 0.9 copy.9
  389.2 1.0 copy.10
  390.2 255.4 %all-reduce.6.cloned.1.call-done = (f32[256,1024]{0,1:T(8,128)}, f32[256,64]{0,1:T(8,128)}) async-done(((f32[256,1024]{0,1:T(8,128)}, f32[256,64]{0,1:T(8,128)}), (f32[256,1024]{0,1:T(8,128)}, f32[256,64]{0,1:T(8,128)})) %all-reduce.6.cloned.1.call-update) | async-done | bytes 1114128 | tf_op jit(solution)/shard_map/psum | solution.py:75
  645.6 0.7 dynamic-slice_add_fusion
  646.3 0.0 copy-done.1
  646.3 1.5 bitcast_divide_fusion
Async XLA Ops:
  7.2 30.5 %copy-start = (bf16[256,1024]{1,0:T(8,128)(2,1)S(1)}, bf16[256,1024]{1,0:T(8,128)(2,1)}, u32[]{:S(2)}) copy-start(bf16[256,1024]{1,0:T(8,128)(2,1)} %param.3) | copy-start | bytes 1572868
  7.2 302.0 %all-reduce.4.cloned.1.call-start = ((), (), s32[]{:S(2)}) async-start(), calls=%async_computation.1 | async-start | bytes 8388608 | tf_op jit(solution)/shard_map/psum | solution.py:65
  40.3 0.8 copy-start.2
  40.3 605.3 %all-reduce.6.cloned.1.call-start = ((), (), s32[]{:S(2)}) async-start(), calls=%async_computation.2 | async-start | bytes 2228224 | tf_op jit(solution)/shard_map/psum | solution.py:75
  381.9 264.4 %copy-start.1 = (bf16[256,64]{0,1:T(8,128)(2,1)S(1)}, bf16[256,64]{0,1:T(8,128)(2,1)}, u32[]{:S(2)}) copy-start(bf16[256,64]{0,1:T(8,128)(2,1)} %param.5) | copy-start | bytes 98308
Sparse Core Ops, SparseCore 0:
  40.5 268.7 all-reduce.3
  387.1 258.4 all-reduce.5
